TPU v7x, 256 devices: a whole 4x4x8 slice. The times are simulated.
256 devices in a mesh: rep: 2 (over core), ep: 128 (over z, y, x).
Axes of the slice: x: 4, y: 4, z: 8, core: 2. Of those that a mesh axis runs over, the one named last changes fastest.
Arguments:
- resid_in: bfloat16 [16384, 2048], P(('rep', 'ep')), may hold values from -6 to 6
- context: bfloat16 [16384, 2048], P('rep', 'ep'), may hold values from -24 to 24
- out_proj: bfloat16 [2048, 2048], P('ep'), may hold values from -0.125 to 0.125
- norm_gain: float32 [2048], replicated, may hold values from 0.5 to 1.5
- router: bfloat16 [2048, 64], replicated, may hold values from -0.03125 to 0.03125
- routes: int32 [16384, 8], P(('rep', 'ep')), may hold values from 0 to 63, all different within a row; in each aligned block of 64 rows (0 to 63, 64 to 127, ...) at most 10 rows name the same one
- w_gate: bfloat16 [2048, 65536], P(None, ('rep', 'ep')), may hold values from -0.125 to 0.125
- w_up: bfloat16 [2048, 65536], P(None, ('rep', 'ep')), may hold values from -0.125 to 0.125
- w_down: bfloat16 [65536, 2048], P(('rep', 'ep')), may hold values from -0.5 to 0.5
- next_gain: float32 [2048], replicated, may hold values from 0.5 to 1.5
Outputs:
- resid_out: bfloat16 [16384, 2048], P(('rep', 'ep'))
- next_normed: bfloat16 [16384, 2048], P(('rep', 'ep'))
Inputs may be any that keep to these rules, and one draw needn't show every extreme that they name: `routes`: each row names 8 different experts. Among the 64 rows of one device no expert is named by more than 10 rows, a bound that some block reaches.
All inputs are finite; a program needn't handle non-finite values.
Results may differ from a plain program's by a relative error of at most 0.014.
Values may be sent and summed in bfloat16 or wider, within the bound.
No kernel may reach another device: no remote copies, remote signals or barrier semaphores. Data moves between devices by JAX's collectives and lax.ppermute only.
A program may use at most 192 MiB of HBM per device.

v0:
```python
import jax
import jax.numpy as jnp
from jax import lax
from jax.sharding import PartitionSpec as P

FF_E = 1024
MOST = 10


def rms_norm(values, gain_row):
    widened = values.astype(jnp.float32)
    factor = lax.rsqrt(jnp.mean(widened * widened, axis=-1, keepdims=True) + 1e-06)
    return (widened * factor * gain_row).astype(jnp.bfloat16)


def body(resid_in, context, out_proj, norm_gain, router, routes, w_gate, w_up, w_down, next_gain):
    model_width = resid_in.shape[1]
    rep_count = lax.axis_size("rep")
    ep_count = lax.axis_size("ep")
    token_ctx = lax.all_to_all(context, "ep", split_axis=0, concat_axis=1, tiled=True)
    attention = jnp.dot(
        token_ctx,
        lax.all_gather(out_proj, "ep", axis=0, tiled=True),
        preferred_element_type=jnp.float32,
    )
    hidden = (resid_in.astype(jnp.float32) + attention).astype(jnp.bfloat16)
    normed = rms_norm(hidden, norm_gain)
    logits = jnp.dot(normed, router, preferred_element_type=jnp.float32)
    experts = router.shape[1]
    picked_mask = (
        routes[:, :, None] == jnp.arange(experts, dtype=jnp.int32)[None, None, :]
    ).astype(jnp.int32)
    picked = jnp.sum(picked_mask.astype(jnp.float32) * logits[:, None, :], axis=2)
    raised = jnp.exp(picked)
    route_weight = (raised / jnp.sum(raised, axis=1, keepdims=True)).astype(jnp.bfloat16)
    units = w_gate.shape[1]
    owners = max(FF_E // units, 1)
    per_device = max(units // FF_E, 1)
    block_size = min(units, FF_E)
    named_count = jnp.sum(picked_mask, axis=1)
    before = jnp.cumsum(named_count, axis=0) - named_count
    order_rank = jnp.sum(picked_mask * before[:, None, :], axis=2)
    owner_part = jnp.arange(owners, dtype=jnp.int32)
    target = (routes[:, :, None] * owners + owner_part[None, None, :]) // per_device
    local_expert = (routes % per_device)[:, :, None]
    slot_width = per_device * MOST
    slot_index = target * slot_width + local_expert * MOST + order_rank[:, :, None]
    slot_total = rep_count * ep_count * slot_width
    slot_hits = slot_index[None] == jnp.arange(slot_total, dtype=jnp.int32)[:, None, None, None]
    pair_hits = jnp.any(slot_hits, axis=3)
    placing = jnp.any(pair_hits, axis=2).astype(jnp.bfloat16)
    outgoing = jnp.dot(placing, normed, preferred_element_type=jnp.bfloat16)
    outgoing = outgoing.reshape(rep_count, ep_count, slot_width, model_width)
    arrived = lax.all_to_all(
        lax.all_to_all(outgoing, "rep", split_axis=0, concat_axis=0, tiled=True),
        "ep",
        split_axis=1,
        concat_axis=1,
        tiled=True,
    )
    slot_rows = arrived.reshape(rep_count * ep_count, per_device, MOST, model_width)
    gate_local = w_gate.reshape(model_width, per_device, block_size)
    up_local = w_up.reshape(model_width, per_device, block_size)
    down_local = w_down.reshape(per_device, block_size, model_width)
    gate_h = jnp.einsum("spmd,dpf->spmf", slot_rows, gate_local, preferred_element_type=jnp.float32)
    up_h = jnp.einsum("spmd,dpf->spmf", slot_rows, up_local, preferred_element_type=jnp.float32)
    activated = (jax.nn.silu(gate_h) * up_h).astype(jnp.bfloat16)
    produced = jnp.einsum(
        "spmf,pfd->spmd", activated, down_local, preferred_element_type=jnp.float32
    ).astype(jnp.bfloat16)
    produced = produced.reshape(rep_count, ep_count, slot_width, model_width)
    returned = lax.all_to_all(
        lax.all_to_all(produced, "rep", split_axis=0, concat_axis=0, tiled=True),
        "ep",
        split_axis=1,
        concat_axis=1,
        tiled=True,
    )
    returned = returned.reshape(slot_total, model_width)
    weighing = jnp.einsum(
        "stk,tk->ts", pair_hits.astype(jnp.float32), route_weight.astype(jnp.float32)
    ).astype(jnp.bfloat16)
    expert_sum = jnp.dot(weighing, returned, preferred_element_type=jnp.float32)
    resid_out = (hidden.astype(jnp.float32) + expert_sum).astype(jnp.bfloat16)
    next_normed = rms_norm(resid_out, next_gain)
    return (resid_out, next_normed)


def solution(mesh):
    in_specs = (
        P(("rep", "ep"), None),
        P("rep", "ep"),
        P("ep", None),
        P(),
        P(),
        P(("rep", "ep"), None),
        P(None, ("rep", "ep")),
        P(None, ("rep", "ep")),
        P(("rep", "ep"), None),
        P(),
    )
    out_specs = (P(("rep", "ep"), None), P(("rep", "ep"), None))
    return jax.shard_map(body, mesh=mesh, in_specs=in_specs, out_specs=out_specs, check_vma=False)
```

profile of v0, /device:TPU:1, one launch (start us, length us, event | category | flops | bytes accessed | tf_op | source)
XLA Modules:
  0.0 805.6 jit_solution(2653581265506161972)
XLA Ops:
  7.9 1.5 all_to_all.26
  9.7 1.0 reshape.89
  10.7 16.8 %all-to-all-start = ((bf16[128,2,512]{2,1,0:T(2,128)(2,1)}), bf16[128,2,512]{2,1,0:T(2,128)(2,1)S(1)}, u32[]{:S(2)}, u32[]{:S(2)}) async-start(bf16[128,2,512]{2,1,0:T(2,128)(2,1)} %reshape.89), calls=%async_computation | async-start | bytes 524288 | tf_op jit(solution)/shard_map/all_to_all | solution.py:20
  29.4 1.2 select_reduce_fusion
  30.7 11.4 %fusion.1 = (pred[2560,64,8]{0,2,1:T(8,128)(4,1)}, pred[2560,64]{0,1:T(8,128)(4,1)S(1)}) fusion(s32[64,8,4]{1,2,0:T(4,128)S(1)} %multiply_add_fusion), kind=kLoop, calls=%fused_computation.2 | loop fusion | flops 14254080 | bytes 1482752 | tf_op jit(solution)/shard_map/reduce_or | solution.py:50
  43.3 92.8 %all-gather.2.cloned.1.call-done = bf16[2048,2048]{1,0:T(8,128)(2,1)} async-done(((bf16[16,2048]{1,0:T(8,128)(2,1)}), bf16[2048,2048]{1,0:T(8,128)(2,1)}) %all-gather.2.cloned.1.call-update) | async-done | bytes 8388624 | tf_op jit(solution)/shard_map/all_gather | solution.py:23
  136.1 5.1 multiply_reduce_fusion
  141.2 3.2 fusion.11
  144.4 16.0 %all_to_all.39 = bf16[2,128,10,2048]{3,1,2,0:T(8,128)(2,1)S(1)} all-to-all(bf16[2,128,10,2048]{3,1,2,0:T(8,128)(2,1)S(1)} %fusion.11), channel_id=1, replica_groups=mesh['rep'=2,'ep'=128] {'rep'}, dimensions={0} | all-to-all | bytes 20971520 | tf_op jit(solution)/shard_map/all_to_all | solution.py:55
  160.4 21.4 %copy.55 = bf16[2,128,10,2048]{3,0,2,1:T(2,128)(2,1)S(1)} copy(bf16[2,128,10,2048]{3,1,2,0:T(8,128)(2,1)S(1)} %all_to_all.39) | data formatting | bytes 20971520 | tf_op jit(solution)/shard_map/all_to_all | solution.py:55
  181.7 239.2 %all_to_all.40 = bf16[2,128,10,2048]{3,0,2,1:T(2,128)(2,1)} all-to-all(bf16[2,128,10,2048]{3,0,2,1:T(2,128)(2,1)S(1)} %copy.55), channel_id=1, replica_groups=mesh['rep'=2,'ep'=128] {'ep'}, dimensions={1} | all-to-all | bytes 20971520 | tf_op jit(solution)/shard_map/all_to_all | solution.py:54
  420.9 13.8 %copy.56 = bf16[2,128,10,2048]{3,1,0,2:T(8,128)(2,1)} copy(bf16[2,128,10,2048]{3,0,2,1:T(2,128)(2,1)} %all_to_all.40) | data formatting | bytes 20971520 | tf_op jit(solution)/shard_map/all_to_all | solution.py:54
  434.8 8.4 %fusion.14 = f32[256,10,256]{2,0,1:T(8,128)} fusion(bf16[256,10,2048]{2,0,1:T(8,128)(2,1)} %bitcast.84, bf16[2048,256]{1,0:T(8,128)(2,1)S(1)} %copy-done.8), kind=kOutput, calls=%fused_computation.21 | convolution fusion | flops 2684354560 | bytes 14155776 | tf_op jit(solution)/shard_map/spmd,dpf->spmf/dot_general | solution.py:66
  443.2 16.5 %convolution_convert_fusion = bf16[256,10,2048]{2,0,1:T(8,128)(2,1)} fusion(f32[256,10,256]{2,0,1:T(8,128)} %fusion.14, bf16[256,10,2048]{2,0,1:T(8,128)(2,1)} %bitcast.85, bf16[256,2048]{1,0:T(8,128)(2,1)S(1)} %copy-done, bf16[2048,256]{1,0:T(8,128)(2,1)} %param.16), kind=kOutput, calls=%fused_computation.3 | convolution fusion | flops 5377884160 | bytes 25690112 | tf_op jit(solution)/shard_map/spmf,pfd->spmd/dot_general | solution.py:68
  459.7 10.2 %copy.57 = bf16[2,128,10,2048]{3,1,2,0:T(8,128)(2,1)} copy(bf16[2,128,10,2048]{3,1,0,2:T(8,128)(2,1)} %bitcast.86) | data formatting | bytes 20971520 | tf_op jit(solution)/shard_map/reshape | solution.py:71
  469.9 17.3 %all_to_all.41 = bf16[2,128,10,2048]{3,1,2,0:T(8,128)(2,1)S(1)} all-to-all(bf16[2,128,10,2048]{3,1,2,0:T(8,128)(2,1)} %copy.57), channel_id=1, replica_groups=mesh['rep'=2,'ep'=128] {'rep'}, dimensions={0} | all-to-all | bytes 20971520 | tf_op jit(solution)/shard_map/all_to_all | solution.py:73
  487.2 29.4 %copy.58 = bf16[2,128,10,2048]{3,0,2,1:T(2,128)(2,1)} copy(bf16[2,128,10,2048]{3,1,2,0:T(8,128)(2,1)S(1)} %all_to_all.41) | data formatting | bytes 20971520 | tf_op jit(solution)/shard_map/all_to_all | solution.py:73
  516.6 7.9 all-to-all-start.4
  525.2 1.7 fusion.27
  526.9 232.2 %all-to-all-done.4 = bf16[2,128,10,2048]{3,0,2,1:T(2,128)(2,1)} async-done(((bf16[2,128,10,2048]{3,0,2,1:T(2,128)(2,1)}), bf16[2,128,10,2048]{3,0,2,1:T(2,128)(2,1)}, u32[]{:S(2)}, u32[]{:S(2)}) %all-to-all-start.4) | async-done | bytes 10485792 | tf_op jit(solution)/shard_map/all_to_all | solution.py:72
  759.1 14.1 %copy.59 = bf16[2,128,10,2048]{3,2,1,0:T(8,128)(2,1)} copy(bf16[2,128,10,2048]{3,0,2,1:T(2,128)(2,1)} %all-to-all-done.4) | data formatting | bytes 20971520 | tf_op jit(solution)/shard_map/all_to_all | solution.py:72
  773.3 18.2 %reshape.82 = bf16[2560,2048]{1,0:T(8,128)(2,1)} reshape(bf16[2,128,10,2048]{3,2,1,0:T(8,128)(2,1)} %copy.59) | data formatting | bytes 20971520 | tf_op jit(solution)/shard_map/reshape | solution.py:79
  791.5 6.1 fusion.18
  797.6 0.8 fusion.20
  (40 shorter events, 4.9 us)
Async XLA Ops:
  7.2 436.0 %copy-start = (bf16[256,2048]{1,0:T(8,128)(2,1)S(1)}, bf16[256,2048]{1,0:T(8,128)(2,1)}, u32[]{:S(2)}) copy-start(bf16[256,2048]{1,0:T(8,128)(2,1)} %param.18) | copy-start | bytes 3145732
  7.2 128.9 %all-gather.2.cloned.1.call-start = ((), (), s32[]{:S(2)}) async-start(), calls=%async_computation.5 | async-start | bytes 8454144 | tf_op jit(solution)/shard_map/all_gather | solution.py:23
  10.7 32.2 %all-to-all-start = ((bf16[128,2,512]{2,1,0:T(2,128)(2,1)}), bf16[128,2,512]{2,1,0:T(2,128)(2,1)S(1)}, u32[]{:S(2)}, u32[]{:S(2)}) async-start(bf16[128,2,512]{2,1,0:T(2,128)(2,1)} %reshape.89), calls=%async_computation | async-start | bytes 524288 | tf_op jit(solution)/shard_map/all_to_all | solution.py:20
  27.6 113.6 %copy-start.6 = (f32[2048]{0:T(1024)S(1)}, f32[2048]{0:T(1024)}, u32[]{:S(2)}) copy-start(f32[2048]{0:T(1024)} %param.13) | copy-start | bytes 24580
  420.9 13.9 %copy-start.8 = (bf16[2048,256]{1,0:T(8,128)(2,1)S(1)}, bf16[2048,256]{1,0:T(8,128)(2,1)}, u32[]{:S(2)}) copy-start(bf16[2048,256]{1,0:T(8,128)(2,1)} %param.17) | copy-start | bytes 3145732
  516.6 7.9 copy-start.5
  516.6 8.6 %copy-start.2 = (pred[2560,64,8]{0,2,1:T(8,128)(4,1)S(1)}, pred[2560,64,8]{0,2,1:T(8,128)(4,1)}, u32[]{:S(2)}) copy-start(pred[2560,64,8]{0,2,1:T(8,128)(4,1)} %get-tuple-element.2) | copy-start | bytes 3932164
  516.6 242.5 %all-to-all-start.4 = ((bf16[2,128,10,2048]{3,0,2,1:T(2,128)(2,1)}), bf16[2,128,10,2048]{3,0,2,1:T(2,128)(2,1)}, u32[]{:S(2)}, u32[]{:S(2)}) async-start(bf16[2,128,10,2048]{3,0,2,1:T(2,128)(2,1)} %copy.58), calls=%async_computation.4 | async-start | bytes 20971520 | tf_op jit(solution)/shard_map/all_to_all | solution.py:72
  773.3 18.2 %copy-start.4 = (bf16[64,1,2560]{2,1,0:T(2,128)(2,1)S(1)}, bf16[64,1,2560]{2,1,0:T(2,128)(2,1)}, u32[]{:S(2)}) copy-start(bf16[64,1,2560]{2,1,0:T(2,128)(2,1)} %fusion.27) | copy-start | bytes 983044
  773.3 25.2 %copy-start.1 = (bf16[256,2048]{1,0:T(8,128)(2,1)S(1)}, bf16[256,2048]{1,0:T(8,128)(2,1)}, u32[]{:S(2)}) copy-start(bf16[256,2048]{1,0:T(8,128)(2,1)} %param.18) | copy-start | bytes 3145732
  791.5 6.1 copy-start.7
  797.6 0.9 copy-start.3
Sparse Core Ops, SparseCore 0:
  11.6 124.4 all-gather.1
where the time goes:
time: 810 us; the launch traced here: 806 us
  waiting for transfers between devices  326 us (40%)
  blocking collectives  272 us (34%)
  local copies, waits for them, and re-layouts  112 us (14%)
  matrix products  41.2 us (5%)
  starting transfers between devices  24.8 us (3%)
  other arithmetic  14.7 us (2%)
  between operations  14.5 us (2%)
    all_to_all x1, blocking collectives, body(): lax.all_to_all(lax.all_to_all(outgoing, 'rep', split_axis=0, concat_axis=...  239 us
    all_to_all x1, waiting for transfers between devices, body(): lax.all_to_all(lax.all_to_all(produced, 'rep', split_axis=0, concat_axis=...  232 us
    all_gather x1, waiting for transfers between devices, body(): lax.all_gather(out_proj, 'ep', axis=0, tiled=True)  92.8 us
    all_to_all x1, local copies, waits for them, and re-layouts, body(): lax.all_to_all(produced, 'rep', split_axis=0, concat_axis=0, tiled=True)  29.4 us
    all_to_all x1, local copies, waits for them, and re-layouts, body(): lax.all_to_all(outgoing, 'rep', split_axis=0, concat_axis=0, tiled=True)  21.4 us
    reshape x1, local copies, waits for them, and re-layouts, body(): returned = returned.reshape(slot_total, model_width)  18.2 us
    all_to_all x1, blocking collectives, body(): lax.all_to_all(produced, 'rep', split_axis=0, concat_axis=0, tiled=True)  17.3 us
    all_to_all x1, starting transfers between devices, body(): lax.all_to_all(context, 'ep', split_axis=0, concat_axis=1, tiled=True)  16.8 us
  transfers between devices with their start and end apart: 3, of which 2 were waited for; matrix products, arithmetic and copies ran while one was open for 2% of the time, Pallas kernels for 0%

commit v1 on v0

v1 whole, which is shorter than its diff:
```python
import jax
import jax.numpy as jnp
from jax import lax
from jax.sharding import Mesh
from jax.sharding import PartitionSpec as P

FF_E = 1024
MOST = 10


def rms_norm(values, gain_row):
    widened = values.astype(jnp.float32)
    factor = lax.rsqrt(jnp.mean(widened * widened, axis=-1, keepdims=True) + 1e-06)
    return (widened * factor * gain_row).astype(jnp.bfloat16)


def body(resid_in, context, out_proj, norm_gain, router, routes, w_gate, w_up, w_down, next_gain):
    model_width = resid_in.shape[1]
    tokens = resid_in.shape[0]
    rep_count = lax.axis_size("rep")
    rep_id = lax.axis_index("rep")

    token_ctx = lax.all_to_all(context, ("grp", "q"), split_axis=0, concat_axis=1, tiled=True)
    half = model_width // rep_count
    proj_half = lax.dynamic_slice_in_dim(out_proj, rep_id * half, half, axis=1)
    proj_cols = lax.all_gather(proj_half, ("grp", "q"), axis=0, tiled=True)
    chip_ctx = lax.all_gather(token_ctx, "rep", axis=0, tiled=True)
    att_cols = jnp.dot(chip_ctx, proj_cols, preferred_element_type=jnp.float32)
    att_cols = att_cols.reshape(rep_count, tokens, half)
    attention = lax.all_to_all(att_cols, "rep", split_axis=0, concat_axis=2, tiled=True)
    attention = attention.reshape(tokens, model_width)

    hidden = (resid_in.astype(jnp.float32) + attention).astype(jnp.bfloat16)
    normed = rms_norm(hidden, norm_gain)
    logits = jnp.dot(normed, router, preferred_element_type=jnp.float32)
    experts = router.shape[1]
    picked_mask = (
        routes[:, :, None] == jnp.arange(experts, dtype=jnp.int32)[None, None, :]
    ).astype(jnp.int32)
    picked = jnp.sum(picked_mask.astype(jnp.float32) * logits[:, None, :], axis=2)
    raised = jnp.exp(picked)
    route_weight = (raised / jnp.sum(raised, axis=1, keepdims=True)).astype(jnp.bfloat16)

    named_count = jnp.sum(picked_mask, axis=1)
    before = jnp.cumsum(named_count, axis=0) - named_count
    order_rank = jnp.sum(picked_mask * before[:, None, :], axis=2)
    slot_index = routes * MOST + order_rank
    slot_total = experts * MOST
    slot_hits = slot_index[None] == jnp.arange(slot_total, dtype=jnp.int32)[:, None, None]
    placing = jnp.any(slot_hits, axis=2).astype(jnp.bfloat16)
    outgoing = jnp.dot(placing, normed, preferred_element_type=jnp.bfloat16)
    outgoing = outgoing.reshape(experts, MOST, model_width)
    arrived = lax.all_to_all(outgoing, ("rep", "grp"), split_axis=0, concat_axis=0, tiled=True)
    rows = arrived.reshape(-1, model_width)

    gate_full = lax.all_gather(w_gate, "q", axis=1, tiled=True)
    up_full = lax.all_gather(w_up, "q", axis=1, tiled=True)
    down_full = lax.all_gather(w_down, "q", axis=0, tiled=True)
    block_size = w_gate.shape[1]
    block_count = FF_E // block_size
    gate_h = jnp.dot(rows, gate_full, preferred_element_type=jnp.float32)
    up_h = jnp.dot(rows, up_full, preferred_element_type=jnp.float32)
    activated = (jax.nn.silu(gate_h) * up_h).astype(jnp.bfloat16)
    produced = jnp.einsum(
        "sbf,bfd->sbd",
        activated.reshape(-1, block_count, block_size),
        down_full.reshape(block_count, block_size, model_width),
        preferred_element_type=jnp.float32,
    ).astype(jnp.bfloat16)
    summed = jnp.sum(produced.astype(jnp.float32), axis=1).astype(jnp.bfloat16)
    summed = summed.reshape(experts, MOST, model_width)
    returned = lax.all_to_all(summed, ("rep", "grp"), split_axis=0, concat_axis=0, tiled=True)
    returned = returned.reshape(slot_total, model_width)

    weighing = jnp.sum(
        slot_hits.astype(jnp.float32) * route_weight.astype(jnp.float32)[None], axis=2
    ).T.astype(jnp.bfloat16)
    expert_sum = jnp.dot(weighing, returned, preferred_element_type=jnp.float32)
    resid_out = (hidden.astype(jnp.float32) + expert_sum).astype(jnp.bfloat16)
    next_normed = rms_norm(resid_out, next_gain)
    return (resid_out, next_normed)


def solution(mesh):
    rep_count = mesh.shape["rep"]
    ep_count = mesh.shape["ep"]
    units = 65536 // (rep_count * ep_count)
    owners = max(FF_E // units, 1)
    devices = mesh.devices.reshape(rep_count, ep_count // owners, owners)
    grid = Mesh(devices, ("rep", "grp", "q"))
    tok = ("rep", "grp", "q")
    feat = ("grp", "q")
    in_specs = (
        P(tok, None),
        P("rep", feat),
        P(feat, None),
        P(),
        P(),
        P(tok, None),
        P(None, tok),
        P(None, tok),
        P(tok, None),
        P(),
    )
    out_specs = (P(tok, None), P(tok, None))
    return jax.shard_map(body, mesh=grid, in_specs=in_specs, out_specs=out_specs, check_vma=False)
```

time: 810 us -> 422 us (0.52)
  blocking collectives: 272 us -> 13.1 us
  local copies, waits for them, and re-layouts: 112 us -> 20.5 us
  matrix products: 41.2 us -> 24.2 us
  waiting for transfers between devices: 326 us -> 310 us
  other arithmetic: 14.7 us -> 3.75 us
  starting transfers between devices: 24.8 us -> 35.6 us
    all_to_all x3 -> x1, blocking collectives: 272 us -> 8.54 us  [body(): lax.all_to_all(att_cols, 'rep', split_axis=0, concat_axis=2, tiled=True)]
    all_to_all x6 -> x4, local copies, waits for them, and re-layouts: 80.6 us -> 2.43 us  [the longest x3 2.03 us: body(): lax.all_to_all(context, ('grp', 'q'), split_axis=0, concat_axis=1, tiled=...]
    all_to_all x2 -> x3, waiting for transfers between devices: 232 us -> 197 us  [the longest x1 93.4 us: body(): lax.all_to_all(outgoing, ('rep', 'grp'), split_axis=0, concat_axis=0, til...]
    all_gather x1 -> x4, waiting for transfers between devices: 92.8 us -> 111 us  [the longest x1 81.1 us: body(): proj_cols = lax.all_gather(proj_half, ('grp', 'q'), axis=0, tiled=True)]
    reshape x1, local copies, waits for them, and re-layouts: 18.2 us -> 4.08 us  [body(): returned = returned.reshape(slot_total, model_width)]
    reduce_or x1, other arithmetic: 11.4 us -> 0.48 us  [body(): placing = jnp.any(slot_hits, axis=2).astype(jnp.bfloat16)]
    all_to_all x2 -> x3, starting transfers between devices: 24.7 us -> 35.3 us  [the longest x1 16.3 us: body(): lax.all_to_all(context, ('grp', 'q'), split_axis=0, concat_axis=1, tiled=...]
    dot_general x4, matrix products: 31.7 us -> 22.4 us  [the longest x1 7.11 us: body(): up_h = jnp.dot(rows, up_full, preferred_element_type=jnp.float32)]
  transfers between devices with their start and end apart: 3 -> 7, of which waited for: 2 -> 5; matrix products, arithmetic and copies ran while one was open for 2% -> 7% of each run, Pallas kernels for 0% -> 0%
where the time goes in v1:
time: 422 us; the launch traced here: 421 us
  waiting for transfers between devices  310 us (73%)
  starting transfers between devices  35.6 us (8%)
  matrix products  24.2 us (6%)
  local copies, waits for them, and re-layouts  20.5 us (5%)
  between operations  14 us (3%)
  blocking collectives  13.1 us (3%)
    all_to_all x1, waiting for transfers between devices, body(): lax.all_to_all(outgoing, ('rep', 'grp'), split_axis=0, concat_axis=0, til...  93.4 us
    all_to_all x1, waiting for transfers between devices, body(): lax.all_to_all(summed, ('rep', 'grp'), split_axis=0, concat_axis=0, tiled...  92.8 us
    all_gather x1, waiting for transfers between devices, body(): proj_cols = lax.all_gather(proj_half, ('grp', 'q'), axis=0, tiled=True)  81.1 us
    all_gather x1, waiting for transfers between devices, body(): down_full = lax.all_gather(w_down, 'q', axis=0, tiled=True)  30 us
    all_to_all x1, starting transfers between devices, body(): lax.all_to_all(context, ('grp', 'q'), split_axis=0, concat_axis=1, tiled=...  16.3 us
    all_to_all x1, starting transfers between devices, body(): lax.all_to_all(summed, ('rep', 'grp'), split_axis=0, concat_axis=0, tiled...  11.1 us
    all_to_all x1, waiting for transfers between devices, body(): lax.all_to_all(context, ('grp', 'q'), split_axis=0, concat_axis=1, tiled=...  11 us
    all_to_all x1, blocking collectives, body(): lax.all_to_all(att_cols, 'rep', split_axis=0, concat_axis=2, tiled=True)  8.54 us
  transfers between devices with their start and end apart: 7, of which 5 were waited for; matrix products, arithmetic and copies ran while one was open for 7% of the time, Pallas kernels for 0%

profile of v1, /device:TPU:1, one launch (start us, length us, event | category | flops | bytes accessed | tf_op | source)
XLA Modules:
  0.0 421.4 jit_solution(16960810240921129613)
XLA Ops:
  7.2 1.4 constant_dynamic-slice_fusion
  10.2 1.5 all_to_all.31
  12.0 1.0 reshape.86
  13.0 16.3 %all-to-all-start = ((bf16[128,2,512]{2,1,0:T(2,128)(2,1)}), bf16[128,2,512]{2,1,0:T(2,128)(2,1)S(1)}, u32[]{:S(2)}, u32[]{:S(2)}) async-start(bf16[128,2,512]{2,1,0:T(2,128)(2,1)} %reshape.86), calls=%async_computation | async-start | bytes 524288 | tf_op jit(solution)/shard_map/all_to_all | solution.py:23
  29.7 1.2 select_reduce_fusion.1
  31.9 11.0 %all-to-all-done = bf16[128,2,512]{2,1,0:T(2,128)(2,1)S(1)} async-done(((bf16[128,2,512]{2,1,0:T(2,128)(2,1)}), bf16[128,2,512]{2,1,0:T(2,128)(2,1)S(1)}, u32[]{:S(2)}, u32[]{:S(2)}) %all-to-all-start) | async-done | bytes 262176 | tf_op jit(solution)/shard_map/all_to_all | solution.py:23
  43.5 4.6 %all_gather.16 = bf16[128,2048]{1,0:T(8,128)(2,1)S(1)} all-gather(bf16[64,2048]{1,0:T(8,128)(2,1)S(1)} %copy.43), channel_id=1, replica_groups=mesh['rep'=2,'grp'=32,'q'=4] {'rep'}, dimensions={0}, use_global_device_ids=true | all-gather | bytes 786432 | tf_op jit(solution)/shard_map/all_gather | solution.py:27
  48.0 81.1 %all-gather.5.cloned.1.call-done = bf16[2048,1024]{1,0:T(8,128)(2,1)} async-done(((bf16[16,1024]{1,0:T(8,128)(2,1)}), bf16[2048,1024]{1,0:T(8,128)(2,1)}) %all-gather.5.cloned.1.call-update) | async-done | bytes 4194320 | tf_op jit(solution)/shard_map/all_gather | solution.py:26
  129.2 2.9 fusion.21
  132.1 8.5 %all_to_all.44 = f32[2,64,1024]{2,1,0:T(8,128)S(1)} all-to-all(f32[2,64,1024]{2,1,0:T(8,128)S(1)} %bitcast.36), channel_id=1, replica_groups=mesh['rep'=2,'grp'=32,'q'=4] {'rep'}, dimensions={0} | all-to-all | bytes 1048576 | tf_op jit(solution)/shard_map/all_to_all | solution.py:30
  141.4 0.9 fusion.10
  142.4 3.5 copy.52
  145.9 7.8 %all-to-all-start.2 = ((bf16[64,10,2048]{2,1,0:T(8,128)(2,1)}), bf16[64,10,2048]{2,1,0:T(8,128)(2,1)}, u32[]{:S(2)}, u32[]{:S(2)}) async-start(bf16[64,10,2048]{2,1,0:T(8,128)(2,1)} %copy.52), calls=%async_computation.2 | async-start | bytes 8388608 | tf_op jit(solution)/shard_map/all_to_all | solution.py:53
  154.3 93.4 %all-to-all-done.2 = bf16[64,10,2048]{2,1,0:T(8,128)(2,1)} async-done(((bf16[64,10,2048]{2,1,0:T(8,128)(2,1)}), bf16[64,10,2048]{2,1,0:T(8,128)(2,1)}, u32[]{:S(2)}, u32[]{:S(2)}) %all-to-all-start.2) | async-done | bytes 2621472 | tf_op jit(solution)/shard_map/all_to_all | solution.py:53
  247.7 4.1 reshape.80
  251.8 6.6 %fusion.20 = f32[640,1024]{1,0:T(8,128)} fusion(bf16[640,2048]{1,0:T(8,128)(2,1)S(1)} %reshape.80, bf16[2048,1024]{1,0:T(8,128)(2,1)} %all-gather.7.cloned.1.call-done), kind=kOutput, calls=%fused_computation.39 | convolution fusion | flops 2684354560 | bytes 9437184 | tf_op jit(solution)/shard_map/dot_general | solution.py:61
  258.4 7.1 %multiply_convert_fusion = bf16[640,1024]{1,0:T(8,128)(2,1)} fusion(f32[640,1024]{1,0:T(8,128)} %fusion.20, bf16[640,2048]{1,0:T(8,128)(2,1)S(1)} %reshape.80, bf16[2048,1024]{1,0:T(8,128)(2,1)} %all-gather.9.cloned.1.call-done), kind=kOutput, calls=%fused_computation.1 | convolution fusion | flops 2688286720 | bytes 10747904 | tf_op jit(solution)/shard_map/dot_general | solution.py:62
  265.5 30.0 %all-gather.11.cloned.1.call-done = bf16[1024,2048]{1,0:T(8,128)(2,1)} async-done(((bf16[256,2048]{1,0:T(8,128)(2,1)}), bf16[1024,2048]{1,0:T(8,128)(2,1)}) %all-gather.11.cloned.1.call-update) | async-done | bytes 4194320 | tf_op jit(solution)/shard_map/all_gather | solution.py:58
  295.5 5.7 %convert_reduce_fusion = bf16[640,2048]{1,0:T(8,128)(2,1)S(1)} fusion(bf16[4,256,2048]{2,1,0:T(8,128)(2,1)} %bitcast.42, bf16[80,4,8,256]{3,2,1,0:T(8,128)(2,1)} %bitcast.43), kind=kOutput, calls=%fused_computation | convolution fusion | flops 2693529600 | bytes 8126464 | tf_op jit(solution)/shard_map/sbf,bfd->sbd/dot_general | solution.py:64
  301.3 2.8 reshape.83
  304.0 11.1 %all-to-all-start.3 = ((bf16[64,10,2048]{2,1,0:T(8,128)(2,1)}), bf16[64,10,2048]{2,1,0:T(8,128)(2,1)}, u32[]{:S(2)}, u32[]{:S(2)}) async-start(bf16[64,10,2048]{2,1,0:T(8,128)(2,1)} %reshape.83), calls=%async_computation.3 | async-start | bytes 8388608 | tf_op jit(solution)/shard_map/all_to_all | solution.py:72
  316.4 92.8 %all-to-all-done.3 = bf16[64,10,2048]{2,1,0:T(8,128)(2,1)} async-done(((bf16[64,10,2048]{2,1,0:T(8,128)(2,1)}), bf16[64,10,2048]{2,1,0:T(8,128)(2,1)}, u32[]{:S(2)}, u32[]{:S(2)}) %all-to-all-start.3) | async-done | bytes 2621472 | tf_op jit(solution)/shard_map/all_to_all | solution.py:72
  409.2 4.1 reshape.84
  414.0 0.8 fusion.6
  (48 shorter events, 6.9 us)
Async XLA Ops:
  7.2 308.0 %copy-start = (bf16[2048,64]{0,1:T(8,128)(2,1)S(1)}, bf16[2048,64]{0,1:T(8,128)(2,1)}, u32[]{:S(2)}) copy-start(bf16[2048,64]{0,1:T(8,128)(2,1)} %param.14) | copy-start | bytes 786436
  7.2 122.0 %all-gather.5.cloned.1.call-start = ((), (), s32[]{:S(2)}) async-start(), calls=%async_computation.4 | async-start | bytes 4227072 | tf_op jit(solution)/shard_map/all_gather | solution.py:26
  8.7 20.7 %copy-start.3 = (s32[64,8]{0,1:T(8,128)S(1)}, s32[64,8]{0,1:T(8,128)}, u32[]{:S(2)}) copy-start(s32[64,8]{0,1:T(8,128)} %param.15) | copy-start | bytes 6148
  8.7 243.2 %all-gather.7.cloned.1.call-start = ((), (), s32[]{:S(2)}) async-start(), calls=%async_computation.5 | async-start | bytes 5242880 | tf_op jit(solution)/shard_map/all_gather | solution.py:56
  9.4 249.0 %all-gather.9.cloned.1.call-start = ((), (), s32[]{:S(2)}) async-start(), calls=%async_computation.6 | async-start | bytes 5242880 | tf_op jit(solution)/shard_map/all_gather | solution.py:57
  13.0 29.9 %all-to-all-start = ((bf16[128,2,512]{2,1,0:T(2,128)(2,1)}), bf16[128,2,512]{2,1,0:T(2,128)(2,1)S(1)}, u32[]{:S(2)}, u32[]{:S(2)}) async-start(bf16[128,2,512]{2,1,0:T(2,128)(2,1)} %reshape.86), calls=%async_computation | async-start | bytes 524288 | tf_op jit(solution)/shard_map/all_to_all | solution.py:23
  132.1 9.1 %copy-start.2 = (bf16[64,2048]{1,0:T(8,128)(2,1)S(1)}, bf16[64,2048]{1,0:T(8,128)(2,1)}, u32[]{:S(2)}) copy-start(bf16[64,2048]{1,0:T(8,128)(2,1)} %param.10) | copy-start | bytes 786436
  132.1 9.3 %copy-start.4 = (f32[2048]{0:T(1024)S(1)}, f32[2048]{0:T(1024)}, u32[]{:S(2)}) copy-start(f32[2048]{0:T(1024)} %param.13) | copy-start | bytes 24580
  145.9 101.8 %all-to-all-start.2 = ((bf16[64,10,2048]{2,1,0:T(8,128)(2,1)}), bf16[64,10,2048]{2,1,0:T(8,128)(2,1)}, u32[]{:S(2)}, u32[]{:S(2)}) async-start(bf16[64,10,2048]{2,1,0:T(8,128)(2,1)} %copy.52), calls=%async_computation.2 | async-start | bytes 8388608 | tf_op jit(solution)/shard_map/all_to_all | solution.py:53
  153.7 141.8 %all-gather.11.cloned.1.call-start = ((), (), s32[]{:S(2)}) async-start(), calls=%async_computation.7 | async-start | bytes 5242880 | tf_op jit(solution)/shard_map/all_gather | solution.py:58
  304.0 105.2 %all-to-all-start.3 = ((bf16[64,10,2048]{2,1,0:T(8,128)(2,1)}), bf16[64,10,2048]{2,1,0:T(8,128)(2,1)}, u32[]{:S(2)}, u32[]{:S(2)}) async-start(bf16[64,10,2048]{2,1,0:T(8,128)(2,1)} %reshape.83), calls=%async_computation.3 | async-start | bytes 8388608 | tf_op jit(solution)/shard_map/all_to_all | solution.py:72
  413.3 0.7 copy-start.5
  414.0 0.9 copy-start.1
Sparse Core Ops, SparseCore 0:
  12.2 116.9 all-gather.4
  130.9 53.2 all-gather.6
  186.0 54.8 all-gather.8
  242.6 52.8 all-gather.10

commit v2 on v1

--- a/solution.py
+++ b/solution.py
@@ -14,18 +14,57 @@
     return (widened * factor * gain_row).astype(jnp.bfloat16)
 
 
+def shift_pairs(size, offset):
+    return [(i, (i + offset) % size) for i in range(size)]
+
+
+def gather_proj(block, sizes):
+    x_n, z_n, y_n = sizes["x"], sizes["z"], sizes["y"]
+    parts = [block] + [lax.ppermute(block, "x", shift_pairs(x_n, d)) for d in range(1, x_n)]
+    block = jnp.stack(parts)
+    parts = [block] + [lax.ppermute(block, "z", shift_pairs(z_n, d)) for d in range(1, z_n)]
+    block = jnp.stack(parts)
+    if y_n == 4:
+        ahead = lax.ppermute(block, "y", shift_pairs(4, 1))
+        behind = lax.ppermute(block, "y", shift_pairs(4, 3))
+        cut = block.shape[0] // 2
+        far_a = lax.ppermute(ahead[:cut], "y", shift_pairs(4, 1))
+        far_b = lax.ppermute(behind[cut:], "y", shift_pairs(4, 3))
+        parts = [block, ahead, jnp.concatenate([far_a, far_b]), behind]
+    else:
+        parts = [block] + [lax.ppermute(block, "y", shift_pairs(y_n, d)) for d in range(1, y_n)]
+    return jnp.stack(parts)
+
+
 def body(resid_in, context, out_proj, norm_gain, router, routes, w_gate, w_up, w_down, next_gain):
     model_width = resid_in.shape[1]
     tokens = resid_in.shape[0]
-    rep_count = lax.axis_size("rep")
+    sizes = {a: lax.axis_size(a) for a in ("rep", "z", "y", "x")}
+    rep_count = sizes["rep"]
     rep_id = lax.axis_index("rep")
+    chip = ("z", "y", "x")
 
-    token_ctx = lax.all_to_all(context, ("grp", "q"), split_axis=0, concat_axis=1, tiled=True)
+    combo = jnp.concatenate([w_gate, w_up, w_down.T], axis=1)
+    combo_all = lax.all_gather(combo, "x", axis=0, tiled=False)
+
+    token_ctx = lax.all_to_all(context, chip, split_axis=0, concat_axis=1, tiled=True)
     half = model_width // rep_count
     proj_half = lax.dynamic_slice_in_dim(out_proj, rep_id * half, half, axis=1)
-    proj_cols = lax.all_gather(proj_half, ("grp", "q"), axis=0, tiled=True)
+    proj_rows = gather_proj(proj_half, sizes)
+    feat_block = proj_half.shape[0]
+    proj_rows = proj_rows.reshape(-1, half)
+    dy = jnp.arange(sizes["y"])[:, None, None]
+    dz = jnp.arange(sizes["z"])[None, :, None]
+    dx = jnp.arange(sizes["x"])[None, None, :]
+    src = (
+        ((lax.axis_index("z") - dz) % sizes["z"]) * (sizes["y"] * sizes["x"])
+        + ((lax.axis_index("y") - dy) % sizes["y"]) * sizes["x"]
+        + (lax.axis_index("x") - dx) % sizes["x"]
+    ).reshape(-1)
     chip_ctx = lax.all_gather(token_ctx, "rep", axis=0, tiled=True)
-    att_cols = jnp.dot(chip_ctx, proj_cols, preferred_element_type=jnp.float32)
+    chip_ctx = chip_ctx.reshape(chip_ctx.shape[0], -1, feat_block)
+    chip_ctx = jnp.take(chip_ctx, src, axis=1).reshape(chip_ctx.shape[0], -1)
+    att_cols = jnp.dot(chip_ctx, proj_rows, preferred_element_type=jnp.float32)
     att_cols = att_cols.reshape(rep_count, tokens, half)
     attention = lax.all_to_all(att_cols, "rep", split_axis=0, concat_axis=2, tiled=True)
     attention = attention.reshape(tokens, model_width)
@@ -50,26 +89,22 @@
     placing = jnp.any(slot_hits, axis=2).astype(jnp.bfloat16)
     outgoing = jnp.dot(placing, normed, preferred_element_type=jnp.bfloat16)
     outgoing = outgoing.reshape(experts, MOST, model_width)
-    arrived = lax.all_to_all(outgoing, ("rep", "grp"), split_axis=0, concat_axis=0, tiled=True)
+    arrived = lax.all_to_all(outgoing, ("rep", "z", "y"), split_axis=0, concat_axis=0, tiled=True)
     rows = arrived.reshape(-1, model_width)
 
-    gate_full = lax.all_gather(w_gate, "q", axis=1, tiled=True)
-    up_full = lax.all_gather(w_up, "q", axis=1, tiled=True)
-    down_full = lax.all_gather(w_down, "q", axis=0, tiled=True)
     block_size = w_gate.shape[1]
-    block_count = FF_E // block_size
-    gate_h = jnp.dot(rows, gate_full, preferred_element_type=jnp.float32)
-    up_h = jnp.dot(rows, up_full, preferred_element_type=jnp.float32)
+    gate_all = combo_all[:, :, :block_size]
+    up_all = combo_all[:, :, block_size:2 * block_size]
+    down_all = combo_all[:, :, 2 * block_size:]
+    gate_h = jnp.einsum("sd,qdj->sqj", rows, gate_all, preferred_element_type=jnp.float32)
+    up_h = jnp.einsum("sd,qdj->sqj", rows, up_all, preferred_element_type=jnp.float32)
     activated = (jax.nn.silu(gate_h) * up_h).astype(jnp.bfloat16)
     produced = jnp.einsum(
-        "sbf,bfd->sbd",
-        activated.reshape(-1, block_count, block_size),
-        down_full.reshape(block_count, block_size, model_width),
-        preferred_element_type=jnp.float32,
+        "sqj,qdj->sqd", activated, down_all, preferred_element_type=jnp.float32
     ).astype(jnp.bfloat16)
     summed = jnp.sum(produced.astype(jnp.float32), axis=1).astype(jnp.bfloat16)
     summed = summed.reshape(experts, MOST, model_width)
-    returned = lax.all_to_all(summed, ("rep", "grp"), split_axis=0, concat_axis=0, tiled=True)
+    returned = lax.all_to_all(summed, ("rep", "z", "y"), split_axis=0, concat_axis=0, tiled=True)
     returned = returned.reshape(slot_total, model_width)
 
     weighing = jnp.sum(
@@ -86,10 +121,11 @@
     ep_count = mesh.shape["ep"]
     units = 65536 // (rep_count * ep_count)
     owners = max(FF_E // units, 1)
-    devices = mesh.devices.reshape(rep_count, ep_count // owners, owners)
-    grid = Mesh(devices, ("rep", "grp", "q"))
-    tok = ("rep", "grp", "q")
-    feat = ("grp", "q")
+    rows_of = 4 if (ep_count // owners) % 4 == 0 else 1
+    devices = mesh.devices.reshape(rep_count, ep_count // owners // rows_of, rows_of, owners)
+    grid = Mesh(devices, ("rep", "z", "y", "x"))
+    tok = ("rep", "z", "y", "x")
+    feat = ("z", "y", "x")
     in_specs = (
         P(tok, None),
         P("rep", feat),

time: 422 us -> 384 us (0.910)
  waiting for transfers between devices: 310 us -> 126 us
  blocking collectives: 13.1 us -> 114 us
  local copies, waits for them, and re-layouts: 20.5 us -> 48.3 us
  starting transfers between devices: 35.6 us -> 47 us
  other arithmetic: 3.75 us -> 12.2 us
    all_gather x4 -> x1, waiting for transfers between devices: 111 us -> 0.02 us  [body(): combo_all = lax.all_gather(combo, 'x', axis=0, tiled=False)]
    all_to_all x3 -> x2, waiting for transfers between devices: 197 us -> 92.8 us  [the longest x1 92.8 us: body(): lax.all_to_all(summed, ('rep', 'z', 'y'), split_axis=0, concat_axis=0, ti...]
    all_to_all x0 -> x1, blocking collectives: none -> 104 us  [body(): lax.all_to_all(outgoing, ('rep', 'z', 'y'), split_axis=0, concat_axis=0,...]
    ppermute x0 -> x14, waiting for transfers between devices: none -> 33.5 us  [the longest x1 17.3 us: gather_proj(): behind = lax.ppermute(block, 'y', shift_pairs(4, 3))]
    ppermute x0 -> x14, starting transfers between devices: none -> 25.2 us  [the longest x7 14.9 us: gather_proj(): lax.ppermute(block, 'z', shift_pairs(z_n, d))]
    all_gather x0 -> x2, local copies, waits for them, and re-layouts: none -> 16.9 us  [the longest x1 16.7 us: body(): combo_all = lax.all_gather(combo, 'x', axis=0, tiled=False)]
    all_to_all x3 -> x2, starting transfers between devices: 35.3 us -> 21.7 us  [the longest x1 15.4 us: body(): lax.all_to_all(context, chip, split_axis=0, concat_axis=1, tiled=True)]
    unnamed x16 -> x36, local copies, waits for them, and re-layouts: 1.63 us -> 6.55 us
  transfers between devices with their start and end apart: 7 -> 17, of which waited for: 5 -> 7; matrix products, arithmetic and copies ran while one was open for 7% -> 8% of each run, Pallas kernels for 0% -> 0%
where the time goes in v2:
time: 384 us; the launch traced here: 383 us
  waiting for transfers between devices  126 us (33%)
  blocking collectives  114 us (30%)
  local copies, waits for them, and re-layouts  48.3 us (13%)
  starting transfers between devices  47 us (12%)
  matrix products  20.7 us (5%)
  between operations  14.5 us (4%)
  other arithmetic  12.2 us (3%)
    all_to_all x1, blocking collectives, body(): lax.all_to_all(outgoing, ('rep', 'z', 'y'), split_axis=0, concat_axis=0,...  104 us
    all_to_all x1, waiting for transfers between devices, body(): lax.all_to_all(summed, ('rep', 'z', 'y'), split_axis=0, concat_axis=0, ti...  92.8 us
    ppermute x1, waiting for transfers between devices, gather_proj(): behind = lax.ppermute(block, 'y', shift_pairs(4, 3))  17.3 us
    all_gather x1, local copies, waits for them, and re-layouts, body(): combo_all = lax.all_gather(combo, 'x', axis=0, tiled=False)  16.7 us
    ppermute x7, waiting for transfers between devices, gather_proj(): lax.ppermute(block, 'z', shift_pairs(z_n, d))  16.2 us
    all_to_all x1, starting transfers between devices, body(): lax.all_to_all(context, chip, split_axis=0, concat_axis=1, tiled=True)  15.4 us
    ppermute x7, starting transfers between devices, gather_proj(): lax.ppermute(block, 'z', shift_pairs(z_n, d))  14.9 us
    dot_general x1, matrix products, body(): jnp.einsum('sqj,qdj->sqd', activated, down_all, preferred_element_type=jn...  11.5 us
  transfers between devices with their start and end apart: 17, of which 7 were waited for; matrix products, arithmetic and copies ran while one was open for 8% of the time, Pallas kernels for 0%

profile of v2, /device:TPU:1, one launch (start us, length us, event | category | flops | bytes accessed | tf_op | source)
XLA Modules:
  0.0 382.7 jit_solution(17358950100011489591)
XLA Ops:
  13.0 3.3 collective-permute-start.2
  19.4 15.4 %all-to-all-start = ((bf16[128,2,512]{2,1,0:T(2,128)(2,1)}), bf16[128,2,512]{2,1,0:T(2,128)(2,1)}, u32[]{:S(2)}, u32[]{:S(2)}) async-start(bf16[128,2,512]{2,1,0:T(2,128)(2,1)} %reshape.262), calls=%async_computation | async-start | bytes 524288 | tf_op jit(solution)/shard_map/all_to_all | solution.py:50
  35.5 2.3 collective-permute-start.4
  37.8 2.7 collective-permute-start.5
  42.1 2.9 collective-permute-start.7
  45.1 3.2 collective-permute-start.8
  50.5 7.3 %collective-permute-done.5 = bf16[4,16,1024]{2,1,0:T(8,128)(2,1)S(1)} collective-permute-done((bf16[4,16,1024]{2,1,0:T(8,128)(2,1)S(1)}, bf16[4,16,1024]{2,1,0:T(8,128)(2,1)S(1)}, u32[]{:S(2)}, u32[]{:S(2)}) %collective-permute-start.5) | collective-permute-done | bytes 131104 | tf_op jit(solution)/shard_map/ppermute | solution.py:25
  57.8 6.8 %collective-permute-done.6 = bf16[4,16,1024]{2,1,0:T(8,128)(2,1)S(1)} collective-permute-done((bf16[4,16,1024]{2,1,0:T(8,128)(2,1)S(1)}, bf16[4,16,1024]{2,1,0:T(8,128)(2,1)S(1)}, u32[]{:S(2)}, u32[]{:S(2)}) %collective-permute-start.6) | collective-permute-done | bytes 131104 | tf_op jit(solution)/shard_map/ppermute | solution.py:25
  66.2 2.4 collective-permute-start.12
  71.8 17.3 %collective-permute-done.12 = bf16[8,4,16,1024]{3,2,1,0:T(8,128)(2,1)S(1)} collective-permute-done((bf16[8,4,16,1024]{3,2,1,0:T(8,128)(2,1)S(1)}, bf16[8,4,16,1024]{3,2,1,0:T(8,128)(2,1)S(1)}, u32[]{:S(2)}, u32[]{:S(2)}) %collective-permute-start.12) | collective-permute-done | bytes 1048608 | tf_op jit(solution)/shard_map/ppermute | solution.py:29
  89.9 3.5 collective-permute-start.13
  100.0 5.1 %all_gather.9 = bf16[128,2048]{1,0:T(8,128)(2,1)S(1)} all-gather(bf16[64,2048]{1,0:T(8,128)(2,1)} %copy.57), channel_id=1, replica_groups=mesh['rep'=2,'z'=8,'y'=4,'x'=4] {'rep'}, dimensions={0}, use_global_device_ids=true | all-gather | bytes 786432 | tf_op jit(solution)/shard_map/all_gather | solution.py:64
  107.1 2.5 select_n.74
  113.3 4.4 %all_to_all.44 = f32[2,64,1024]{2,1,0:T(8,128)S(1)} all-to-all(f32[2,64,1024]{2,1,0:T(8,128)S(1)} %fusion.12), channel_id=1, replica_groups=mesh['rep'=2,'z'=8,'y'=4,'x'=4] {'rep'}, dimensions={0} | all-to-all | bytes 1048576 | tf_op jit(solution)/shard_map/all_to_all | solution.py:69
  121.1 104.2 %all_to_all.45 = bf16[64,10,2048]{2,1,0:T(8,128)(2,1)} all-to-all(bf16[64,10,2048]{2,1,0:T(8,128)(2,1)S(1)} %copy.71), channel_id=1, replica_groups=mesh['rep'=2,'z'=8,'y'=4,'x'=4] {'rep','z','y'}, dimensions={0} | all-to-all | bytes 5242880 | tf_op jit(solution)/shard_map/all_to_all | solution.py:92
  225.2 4.1 %reshape.260 = bf16[640,2048,1]{1,0,2:T(8,128)(2,1)S(1)} reshape(bf16[64,10,2048]{2,1,0:T(8,128)(2,1)} %all_to_all.45) | data formatting | bytes 5242880 | tf_op jit(solution)/shard_map/reshape | solution.py:93
  229.3 16.7 %copy.68 = bf16[8192,768]{1,0:T(8,128)(2,1)} copy(bf16[8192,768]{0,1:T(8,128)(2,1)} %all-gather.3.cloned.1.call-done) | data formatting | bytes 25165824 | tf_op jit(solution)/shard_map/all_gather | solution.py:48
  246.0 6.6 %fusion.2 = f32[640,4,256]{2,0,1:T(8,128)} fusion(bf16[640,2048,1]{1,0,2:T(8,128)(2,1)S(1)} %reshape.260, bf16[4,2048,768]{2,1,0:T(8,128)(2,1)} %bitcast.65), kind=kOutput, calls=%fused_computation.4 | convolution fusion | flops 2684354560 | bytes 9437184 | tf_op jit(solution)/shard_map/sd,qdj->sqj/dot_general | solution.py:99
  252.6 11.5 %convert_reduce_fusion = bf16[2048,640]{1,0:T(8,128)(2,1)} fusion(bf16[4,2048,768]{2,1,0:T(8,128)(2,1)} %bitcast.66, f32[640,4,256]{2,0,1:T(8,128)} %fusion.2, bf16[640,2048,1]{1,0,2:T(8,128)(2,1)S(1)} %reshape.260), kind=kOutput, calls=%fused_computation.1 | convolution fusion | flops 5381816320 | bytes 16252928 | tf_op jit(solution)/shard_map/sqj,qdj->sqd/dot_general | solution.py:102
  264.1 3.0 copy.72
  267.1 2.8 reshape.247
  269.9 6.4 %all-to-all-start.3 = ((bf16[64,10,2048]{2,1,0:T(8,128)(2,1)}), bf16[64,10,2048]{2,1,0:T(8,128)(2,1)}, u32[]{:S(2)}, u32[]{:S(2)}) async-start(bf16[64,10,2048]{2,1,0:T(8,128)(2,1)} %reshape.247), calls=%async_computation.3 | async-start | bytes 8388608 | tf_op jit(solution)/shard_map/all_to_all | solution.py:107
  277.4 92.8 %all-to-all-done.3 = bf16[64,10,2048]{2,1,0:T(8,128)(2,1)} async-done(((bf16[64,10,2048]{2,1,0:T(8,128)(2,1)}), bf16[64,10,2048]{2,1,0:T(8,128)(2,1)}, u32[]{:S(2)}, u32[]{:S(2)}) %all-to-all-start.3) | async-done | bytes 2621472 | tf_op jit(solution)/shard_map/all_to_all | solution.py:107
  370.2 4.1 %reshape.248 = bf16[640,2048]{1,0:T(8,128)(2,1)S(1)} reshape(bf16[64,10,2048]{2,1,0:T(8,128)(2,1)} %all-to-all-done.3) | data formatting | bytes 5242880 | tf_op jit(solution)/shard_map/reshape | solution.py:108
  (110 shorter events, 37.2 us)
Async XLA Ops:
  7.2 269.1 %copy-start = (bf16[2048,64]{0,1:T(8,128)(2,1)S(1)}, bf16[2048,64]{0,1:T(8,128)(2,1)}, u32[]{:S(2)}) copy-start(bf16[2048,64]{0,1:T(8,128)(2,1)} %param.14) | copy-start | bytes 786436
  7.2 222.1 %all-gather.3.cloned.1.call-start = ((), (), s32[]{:S(2)}) async-start(), calls=%async_computation.4 | async-start | bytes 15728640 | tf_op jit(solution)/shard_map/all_gather | solution.py:48
  12.2 5.3 %copy-start.5 = (bf16[8192,16]{0,1:T(8,128)(2,1)S(1)}, bf16[8192,16]{0,1:T(8,128)(2,1)}, u32[]{:S(2)}) copy-start(bf16[8192,16]{0,1:T(8,128)(2,1)} %param.11) | copy-start | bytes 786436
  12.2 56.5 %copy-start.8 = (s32[64,8]{0,1:T(8,128)S(1)}, s32[64,8]{0,1:T(8,128)}, u32[]{:S(2)}) copy-start(s32[64,8]{0,1:T(8,128)} %param.15) | copy-start | bytes 6148
  13.0 21.8 %collective-permute-start.2 = (bf16[16,1024]{1,0:T(8,128)(2,1)S(1)}, bf16[16,1024]{1,0:T(8,128)(2,1)S(1)}, u32[]{:S(2)}, u32[]{:S(2)}) collective-permute-start(bf16[16,1024]{1,0:T(8,128)(2,1)S(1)} %constant_dynamic-slice_fusion), channel_id=1, source_target_pairs={{0,3},{1,0},{2,1},{3,2},{4,7},{5,4},{6,5},{7,6},{8,11},{9,8},{10,9... | collective-permute-start | bytes 98312 | tf_op jit(solution)/shard_map/ppermute | solution.py:23
  16.3 18.5 %collective-permute-start.1 = (bf16[16,1024]{1,0:T(8,128)(2,1)S(1)}, bf16[16,1024]{1,0:T(8,128)(2,1)S(1)}, u32[]{:S(2)}, u32[]{:S(2)}) collective-permute-start(bf16[16,1024]{1,0:T(8,128)(2,1)S(1)} %constant_dynamic-slice_fusion), channel_id=1, source_target_pairs={{0,2},{1,3},{2,0},{3,1},{4,6},{5,7},{6,4},{7,5},{8,10},{9,11},{10,... | collective-permute-start | bytes 98312 | tf_op jit(solution)/shard_map/ppermute | solution.py:23
  16.9 18.0 %collective-permute-start = (bf16[16,1024]{1,0:T(8,128)(2,1)S(1)}, bf16[16,1024]{1,0:T(8,128)(2,1)S(1)}, u32[]{:S(2)}, u32[]{:S(2)}) collective-permute-start(bf16[16,1024]{1,0:T(8,128)(2,1)S(1)} %constant_dynamic-slice_fusion), channel_id=1, source_target_pairs={{0,1},{1,2},{2,3},{3,0},{4,5},{5,6},{6,7},{7,4},{8,9},{9,10},{10,1... | collective-permute-start | bytes 98312 | tf_op jit(solution)/shard_map/ppermute | solution.py:23
  19.4 78.4 %all-to-all-start = ((bf16[128,2,512]{2,1,0:T(2,128)(2,1)}), bf16[128,2,512]{2,1,0:T(2,128)(2,1)}, u32[]{:S(2)}, u32[]{:S(2)}) async-start(bf16[128,2,512]{2,1,0:T(2,128)(2,1)} %reshape.262), calls=%async_computation | async-start | bytes 524288 | tf_op jit(solution)/shard_map/all_to_all | solution.py:50
  34.9 10.2 %collective-permute-start.3 = (bf16[4,16,1024]{2,1,0:T(8,128)(2,1)S(1)}, bf16[4,16,1024]{2,1,0:T(8,128)(2,1)S(1)}, u32[]{:S(2)}, u32[]{:S(2)}) collective-permute-start(bf16[4,16,1024]{2,1,0:T(8,128)(2,1)S(1)} %pad_maximum_fusion.2), channel_id=1, source_target_pairs={{0,16},{16,32},{32,48},{48,64},{64,80},{80,96},{96,112},{112,0},{1... | collective-permute-start | bytes 393224 | tf_op jit(solution)/shard_map/ppermute | solution.py:25
  35.5 13.4 %collective-permute-start.4 = (bf16[4,16,1024]{2,1,0:T(8,128)(2,1)S(1)}, bf16[4,16,1024]{2,1,0:T(8,128)(2,1)S(1)}, u32[]{:S(2)}, u32[]{:S(2)}) collective-permute-start(bf16[4,16,1024]{2,1,0:T(8,128)(2,1)S(1)} %pad_maximum_fusion.2), channel_id=1, source_target_pairs={{0,32},{16,48},{32,64},{48,80},{64,96},{80,112},{96,0},{112,16},{1... | collective-permute-start | bytes 393224 | tf_op jit(solution)/shard_map/ppermute | solution.py:25
  37.8 20.0 %collective-permute-start.5 = (bf16[4,16,1024]{2,1,0:T(8,128)(2,1)S(1)}, bf16[4,16,1024]{2,1,0:T(8,128)(2,1)S(1)}, u32[]{:S(2)}, u32[]{:S(2)}) collective-permute-start(bf16[4,16,1024]{2,1,0:T(8,128)(2,1)S(1)} %pad_maximum_fusion.2), channel_id=1, source_target_pairs={{0,48},{16,64},{32,80},{48,96},{64,112},{80,0},{96,16},{112,32},{1... | collective-permute-start | bytes 393224 | tf_op jit(solution)/shard_map/ppermute | solution.py:25
  40.5 24.2 %collective-permute-start.6 = (bf16[4,16,1024]{2,1,0:T(8,128)(2,1)S(1)}, bf16[4,16,1024]{2,1,0:T(8,128)(2,1)S(1)}, u32[]{:S(2)}, u32[]{:S(2)}) collective-permute-start(bf16[4,16,1024]{2,1,0:T(8,128)(2,1)S(1)} %pad_maximum_fusion.2), channel_id=1, source_target_pairs={{0,64},{16,80},{32,96},{48,112},{64,0},{80,16},{96,32},{112,48},{1... | collective-permute-start | bytes 393224 | tf_op jit(solution)/shard_map/ppermute | solution.py:25
  42.1 22.6 %collective-permute-start.7 = (bf16[4,16,1024]{2,1,0:T(8,128)(2,1)S(1)}, bf16[4,16,1024]{2,1,0:T(8,128)(2,1)S(1)}, u32[]{:S(2)}, u32[]{:S(2)}) collective-permute-start(bf16[4,16,1024]{2,1,0:T(8,128)(2,1)S(1)} %pad_maximum_fusion.2), channel_id=1, source_target_pairs={{0,80},{16,96},{32,112},{48,0},{64,16},{80,32},{96,48},{112,64},{1... | collective-permute-start | bytes 393224 | tf_op jit(solution)/shard_map/ppermute | solution.py:25
  45.1 20.3 %collective-permute-start.8 = (bf16[4,16,1024]{2,1,0:T(8,128)(2,1)S(1)}, bf16[4,16,1024]{2,1,0:T(8,128)(2,1)S(1)}, u32[]{:S(2)}, u32[]{:S(2)}) collective-permute-start(bf16[4,16,1024]{2,1,0:T(8,128)(2,1)S(1)} %pad_maximum_fusion.2), channel_id=1, source_target_pairs={{0,96},{16,112},{32,0},{48,16},{64,32},{80,48},{96,64},{112,80},{1... | collective-permute-start | bytes 393224 | tf_op jit(solution)/shard_map/ppermute | solution.py:25
  48.9 17.3 %collective-permute-start.9 = (bf16[4,16,1024]{2,1,0:T(8,128)(2,1)S(1)}, bf16[4,16,1024]{2,1,0:T(8,128)(2,1)S(1)}, u32[]{:S(2)}, u32[]{:S(2)}) collective-permute-start(bf16[4,16,1024]{2,1,0:T(8,128)(2,1)S(1)} %pad_maximum_fusion.2), channel_id=1, source_target_pairs={{0,112},{16,0},{32,16},{48,32},{64,48},{80,64},{96,80},{112,96},{1... | collective-permute-start | bytes 393224 | tf_op jit(solution)/shard_map/ppermute | solution.py:25
  66.2 31.6 %copy-start.1 = (bf16[8,4,16,1024]{3,2,1,0:T(8,128)(2,1)}, bf16[8,4,16,1024]{3,2,1,0:T(8,128)(2,1)S(1)}, u32[]{:S(2)}) copy-start(bf16[8,4,16,1024]{3,2,1,0:T(8,128)(2,1)S(1)} %bitcast_dynamic-update-slice_fusion) | copy-start | bytes 3145732
  66.2 22.9 %collective-permute-start.12 = (bf16[8,4,16,1024]{3,2,1,0:T(8,128)(2,1)S(1)}, bf16[8,4,16,1024]{3,2,1,0:T(8,128)(2,1)S(1)}, u32[]{:S(2)}, u32[]{:S(2)}) collective-permute-start(bf16[8,4,16,1024]{3,2,1,0:T(8,128)(2,1)S(1)} %bitcast_dynamic-update-slice_fusion), channel_id=1, source_target_pairs={{0,12},{4,0},{8,4},{12,8},{1,13},{5,1},{9,5},{13,9},{2,14},{6,2},{... | collective-permute-start | bytes 3145736 | tf_op jit(solution)/shard_map/ppermute | solution.py:29
  68.6 24.8 %collective-permute-start.10 = (bf16[8,4,16,1024]{3,2,1,0:T(8,128)(2,1)S(1)}, bf16[8,4,16,1024]{3,2,1,0:T(8,128)(2,1)S(1)}, u32[]{:S(2)}, u32[]{:S(2)}) collective-permute-start(bf16[8,4,16,1024]{3,2,1,0:T(8,128)(2,1)S(1)} %bitcast_dynamic-update-slice_fusion), channel_id=1, source_target_pairs={{0,4},{4,8},{8,12},{12,0},{1,5},{5,9},{9,13},{13,1},{2,6},{6,10},{... | collective-permute-start | bytes 3145736 | tf_op jit(solution)/shard_map/ppermute | solution.py:28
  89.9 19.6 %collective-permute-start.13 = (bf16[4,4,16,1024]{3,2,1,0:T(8,128)(2,1)}, bf16[4,4,16,1024]{3,2,1,0:T(8,128)(2,1)}, u32[]{:S(2)}, u32[]{:S(2)}) collective-permute-start(bf16[4,4,16,1024]{3,2,1,0:T(8,128)(2,1)} %slice.23), channel_id=1, source_target_pairs={{0,12},{4,0},{8,4},{12,8},{1,13},{5,1},{9,5},{13,9},{2,14},{6,2},{... | collective-permute-start | bytes 1572872 | tf_op jit(solution)/shard_map/ppermute | solution.py:32
  94.2 15.3 %collective-permute-start.11 = (bf16[4,4,16,1024]{3,2,1,0:T(8,128)(2,1)}, bf16[4,4,16,1024]{3,2,1,0:T(8,128)(2,1)}, u32[]{:S(2)}, u32[]{:S(2)}) collective-permute-start(bf16[4,4,16,1024]{3,2,1,0:T(8,128)(2,1)} %slice.22), channel_id=1, source_target_pairs={{0,4},{4,8},{8,12},{12,0},{1,5},{5,9},{9,13},{13,1},{2,6},{6,10},{... | collective-permute-start | bytes 1572872 | tf_op jit(solution)/shard_map/ppermute | solution.py:31
  113.3 5.1 %copy-start.6 = (bf16[64,2048]{1,0:T(8,128)(2,1)S(1)}, bf16[64,2048]{1,0:T(8,128)(2,1)}, u32[]{:S(2)}) copy-start(bf16[64,2048]{1,0:T(8,128)(2,1)} %param.10) | copy-start | bytes 786436
  113.3 5.2 %copy-start.4 = (pred[64,10,64]{2,1,0:T(8,128)(4,1)S(1)}, pred[64,10,64]{2,1,0:T(8,128)(4,1)}, u32[]{:S(2)}) copy-start(pred[64,10,64]{2,1,0:T(8,128)(4,1)} %dot_general.25) | copy-start | bytes 122884
  113.3 5.2 %copy-start.9 = (f32[2048]{0:T(1024)S(1)}, f32[2048]{0:T(1024)}, u32[]{:S(2)}) copy-start(f32[2048]{0:T(1024)} %param.13) | copy-start | bytes 24580
  269.9 100.4 %all-to-all-start.3 = ((bf16[64,10,2048]{2,1,0:T(8,128)(2,1)}), bf16[64,10,2048]{2,1,0:T(8,128)(2,1)}, u32[]{:S(2)}, u32[]{:S(2)}) async-start(bf16[64,10,2048]{2,1,0:T(8,128)(2,1)} %reshape.247), calls=%async_computation.3 | async-start | bytes 8388608 | tf_op jit(solution)/shard_map/all_to_all | solution.py:107
  (5 other events, 6.3 us)
Sparse Core Ops, SparseCore 0:
  12.3 127.5 all-gather.2
